TPU v7x, 128 devices: a whole 4x4x4 slice. The times are simulated.
128 devices in a mesh: sky: 4 (over y), visit: 32 (over x, z, core).
Axes of the slice: x: 4, y: 4, z: 4, core: 2. Of those that a mesh axis runs over, the one named last changes fastest.
Arguments:
- sky_image: float32 [6, 2048, 16384], P(None, 'sky', 'visit'), may hold values from -6 to 6
- observed: bfloat16 [768, 512, 512], P(('sky', 'visit')), may hold values from -6 to 6
- footprint: int32 [768, 2], P(('sky', 'visit')), may hold values from 0 to 123, as said below
- segment_band: int32 [768], P(('sky', 'visit')), may hold values from 0 to 5
- offsets: int32 [768, 2], P(('sky', 'visit')), may hold values from 0 to 127
- psf_rows: bfloat16 [4, 512, 512], replicated, may hold values from -0.25 to 0.25
- psf_cols: bfloat16 [4, 512, 512], replicated, may hold values from -0.25 to 0.25
- psf_weights: float32 [768, 4], P(('sky', 'visit')), may hold values from 0.2 to 1
- step_sizes: float32 [6], replicated, may hold values from 0.05 to 0.5
Outputs:
- updated_sky: float32 [6, 2048, 16384], P(None, 'sky', 'visit')
Inputs may be any that keep to these rules, and one draw needn't show every extreme that they name: Segment s is held by device s // 6 (row-major over sky then visit, owning the sky block of that position). Its footprint lies inside the sky and within 2 tiles of that device's block on every side; on every device whose block does not touch the sky's border, some segment's footprint starts 2 tiles before the block in rows and columns and some segment's footprint ends 2 tiles after it.
All inputs are finite; a program needn't handle non-finite values.
Results may differ from a plain program's by a relative error of at most 0.0095.
Values may be sent and summed in bfloat16 or wider, within the bound.
No kernel may reach another device: no remote copies, remote signals or barrier semaphores. Data moves between devices by JAX's collectives and lax.ppermute only.
A program may use at most 192 MiB of HBM per device.

v0:
```python
import jax
import jax.numpy as jnp
from jax import lax
from jax.sharding import PartitionSpec as P

TILE = 128


def from_behind(value, axis, by):
    count = lax.axis_size(axis)
    pairs = [(i, i + by) for i in range(count) if 0 <= i + by < count]
    return lax.ppermute(value, axis, pairs)


def extended_2(block, sides, width):
    for axis, dim in sides:
        count = lax.axis_size(axis)
        forward = [(i, i + 1) for i in range(count - 1)]
        backward = [(target, source) for source, target in forward]
        low = lax.ppermute(
            lax.slice_in_dim(block, block.shape[dim] - width, None, axis=dim), axis, forward
        )
        high = lax.ppermute(lax.slice_in_dim(block, 0, width, axis=dim), axis, backward)
        block = jnp.concatenate([low, block, high], axis=dim)
    return block


def fold_cols(canvas, rim_width):
    full_width = canvas.shape[2]
    inner_width = full_width - 2 * rim_width
    interior = canvas[:, :, rim_width : full_width - rim_width]
    arrived = []
    for step_by, rim_strip in (
        (1, canvas[:, :, full_width - rim_width :]),
        (-1, canvas[:, :, :rim_width]),
    ):
        arrived.append(
            from_behind(rim_strip.astype(jnp.bfloat16), "visit", step_by).astype(rim_strip.dtype)
        )
    interior = interior.at[:, :, :rim_width].add(arrived[0])
    interior = interior.at[:, :, inner_width - rim_width :].add(arrived[1])
    return interior


def fold_rows(canvas, rim_width):
    full_height = canvas.shape[1]
    inner_height = full_height - 2 * rim_width
    interior = canvas[:, rim_width : full_height - rim_width, :]
    arrived = []
    for step_by, rim_strip in (
        (1, canvas[:, full_height - rim_width :, :]),
        (-1, canvas[:, :rim_width, :]),
    ):
        arrived.append(
            from_behind(rim_strip.astype(jnp.bfloat16), "sky", step_by).astype(rim_strip.dtype)
        )
    interior = interior.at[:, :rim_width, :].add(arrived[0])
    interior = interior.at[:, inner_height - rim_width :, :].add(arrived[1])
    return interior


def per_device(
    sky_image,
    observed,
    footprint,
    segment_band,
    offsets,
    psf_rows,
    psf_cols,
    psf_weights,
    step_sizes,
):
    block_side = sky_image.shape[1]
    pixels = observed.shape[1]
    term_count = psf_rows.shape[0]
    rim_width = (pixels // TILE + 1) // 2 * TILE
    sky_bf = sky_image.astype(jnp.bfloat16)
    extended = extended_2(sky_bf, (("sky", 1), ("visit", 2)), rim_width)
    row_anchor = lax.axis_index("sky") * block_side - rim_width
    col_anchor = lax.axis_index("visit") * block_side - rim_width
    top_rows = footprint[:, 0] * TILE + offsets[:, 0] - row_anchor
    left_cols = footprint[:, 1] * TILE + offsets[:, 1] - col_anchor
    rows_flat = psf_rows.reshape(term_count * pixels, pixels)

    def visit_segment(canvas_sum, packed):
        target, weights, band_index, top, left_col = packed
        window = lax.dynamic_slice(extended, (band_index, top, left_col), (1, pixels, pixels))[0]
        left_terms = jnp.dot(rows_flat, window, preferred_element_type=jnp.float32).astype(
            jnp.bfloat16
        )
        left_terms = left_terms.reshape(term_count, pixels, pixels)
        blurred = jnp.einsum(
            "kij,klj->kil", left_terms, psf_cols, preferred_element_type=jnp.float32
        )
        model_image = jnp.sum(weights[:, None, None] * blurred, axis=0)
        residual = (model_image - target.astype(jnp.float32)).astype(jnp.bfloat16)
        right_terms = jnp.einsum(
            "ij,kjl->kil", residual, psf_cols, preferred_element_type=jnp.float32
        ).astype(jnp.bfloat16)
        spread = jnp.einsum(
            "kji,kjl->kil", psf_rows, right_terms, preferred_element_type=jnp.float32
        )
        adjoint = jnp.sum(weights[:, None, None] * spread, axis=0).astype(jnp.bfloat16)
        current = lax.dynamic_slice(canvas_sum, (band_index, top, left_col), (1, pixels, pixels))
        canvas_sum = lax.dynamic_update_slice(
            canvas_sum, current + adjoint.astype(jnp.float32)[None], (band_index, top, left_col)
        )
        return (canvas_sum, None)

    empty_sum = jnp.zeros(extended.shape, jnp.float32)
    canvas_sum, unused = lax.scan(
        visit_segment, empty_sum, (observed, psf_weights, segment_band, top_rows, left_cols)
    )
    gradient = fold_rows(fold_cols(canvas_sum, rim_width), rim_width)
    return sky_image - step_sizes[:, None, None] * gradient


def solution(mesh):
    placed = (
        P(None, "sky", "visit"),
        P(("sky", "visit"), None, None),
        P(("sky", "visit"), None),
        P(("sky", "visit")),
        P(("sky", "visit"), None),
        P(),
        P(),
        P(("sky", "visit"), None),
        P(),
    )
    return jax.shard_map(
        per_device, mesh=mesh, in_specs=placed, out_specs=P(None, "sky", "visit"), check_vma=False
    )
```

profile of v0, /device:TPU:104, one launch (start us, length us, event | category | flops | bytes accessed | tf_op | source)
XLA Modules:
  0.0 434.6 jit_solution(10736592764289758982)
XLA Ops:
  9.4 32.1 %collective-permute-done = bf16[6,256,512]{2,1,0:T(8,128)(2,1)S(1)} collective-permute-done((bf16[6,256,512]{2,1,0:T(8,128)(2,1)S(1)}, bf16[6,256,512]{2,1,0:T(8,128)(2,1)S(1)}, u32[]{:S(2)}, u32[]{:S(2)}) %collective-permute-start) | collective-permute-done | bytes 1572896 | tf_op jit(solution)/shard_map/ppermute | solution.py:20
  55.3 33.2 %collective-permute-done.2 = bf16[6,1024,256]{2,1,0:T(8,128)(2,1)} collective-permute-done((bf16[6,1024,256]{2,1,0:T(8,128)(2,1)}, bf16[6,1024,256]{2,1,0:T(8,128)(2,1)}, u32[]{:S(2)}, u32[]{:S(2)}) %collective-permute-start.2) | collective-permute-done | bytes 3145760 | tf_op jit(solution)/shard_map/ppermute | solution.py:20
  90.3 9.6 %pad_maximum_fusion = bf16[6,1024,1024]{2,1,0:T(8,128)(2,1)} fusion(bf16[6,1024,256]{2,1,0:T(8,128)(2,1)} %collective-permute-done.3, bf16[6,256,512]{2,1,0:T(8,128)(2,1)} %copy-done.1, bf16[6,512,512]{2,1,0:T(8,128)(2,1)S(1)} %convert_element_type.68, bf16[6,256,512]{2,1,0:T(8,128)(2,1)} %copy-done, bf16[6,1024,256]{2,1,0:T(8,128)(2,1)} %collective-permute-done.2), kind=kLoop, calls=%fused_computation.17 | loop fusion | flops 62914560 | bytes 25165824 | tf_op jit(solution)/shard_map/concatenate | solution.py:24
  99.9 11.5 %broadcast_in_dim.2.clone = f32[6,1024,1024]{2,1,0:T(8,128)} broadcast(f32[]{:T(128)} %constant.134.clone.1), dimensions={} | broadcast | bytes 25165828 | tf_op jit(solution)/shard_map/broadcast_in_dim | solution.py:110
  111.4 207.4 %while.14 = (s32[]{:T(128)}, f32[6,1024,1024]{2,1,0:T(8,128)}, s32[6]{0:T(128)S(1)}, s32[6]{0:T(128)S(1)}, s32[6]{0:T(128)S(1)}, /*index=5*/f32[6,4]{1,0:T(8,128...) while((s32[]{:T(128)}, f32[6,1024,1024]{2,1,0:T(8,128)}, ...), condition=%wide.region_3.4_spmd, body=%wide.region_0.3_spmd.sunk | while | flops 4302045184 | bytes 31457660 | solution.py:111
  132.6 5.2 %multiply_reduce_fusion.5 = bf16[512,512]{1,0:T(8,128)(2,1)S(1)} fusion(bf16[4,512,512]{2,1,0:T(8,128)(2,1)} %get-tuple-element.272, f32[4]{0:T(128)S(1)} %dynamic-slice_bitcast_fusion.2, bf16[4,512,512]{2,1,0:T(8,128)(2,1)} %get-tuple-element.270, f32[512,512]{1,0:T(8,128)} %multiply_reduce_fusion.4, bf16[6,512,512]{2,1,0:T(8,128)(2,1)} %get-tuple-element.271, ...), kind=kOutput, calls=%fused_computation.clone.1 | convolution fusion | flops 2151153664 | bytes 6291476 | tf_op jit(solution)/shard_map/while/body/eval_jaxpr/kji,kjl->kil/dot_general | solution.py:100
  138.3 7.7 %dynamic_update_slice.4 = f32[6,1024,1024]{2,1,0:T(8,128)} dynamic-update-slice(f32[6,1024,1024]{2,1,0:T(8,128)} %get-tuple-element.248, f32[1,512,512]{2,1,0:T(8,128)S(1)} %copy.25, s32[]{:T(128)S(6)} %select_n.18, s32[]{:T(128)S(6)} %select_n.19, s32[]{:T(128)S(6)} %select_n.20) | dynamic-update-slice | bytes 2097156 | tf_op jit(solution)/shard_map/while/body/eval_jaxpr/dynamic_update_slice | solution.py:105
  167.2 5.2 %multiply_reduce_fusion.5 = bf16[512,512]{1,0:T(8,128)(2,1)S(1)} fusion(bf16[4,512,512]{2,1,0:T(8,128)(2,1)} %get-tuple-element.272, f32[4]{0:T(128)S(1)} %dynamic-slice_bitcast_fusion.2, bf16[4,512,512]{2,1,0:T(8,128)(2,1)} %get-tuple-element.270, f32[512,512]{1,0:T(8,128)} %multiply_reduce_fusion.4, bf16[6,512,512]{2,1,0:T(8,128)(2,1)} %get-tuple-element.271, ...), kind=kOutput, calls=%fused_computation.clone.1 | convolution fusion | flops 2151153664 | bytes 6291476 | tf_op jit(solution)/shard_map/while/body/eval_jaxpr/kji,kjl->kil/dot_general | solution.py:100
  172.8 7.7 %dynamic_update_slice.4 = f32[6,1024,1024]{2,1,0:T(8,128)} dynamic-update-slice(f32[6,1024,1024]{2,1,0:T(8,128)} %get-tuple-element.248, f32[1,512,512]{2,1,0:T(8,128)S(1)} %copy.25, s32[]{:T(128)S(6)} %select_n.18, s32[]{:T(128)S(6)} %select_n.19, s32[]{:T(128)S(6)} %select_n.20) | dynamic-update-slice | bytes 2097156 | tf_op jit(solution)/shard_map/while/body/eval_jaxpr/dynamic_update_slice | solution.py:105
  201.7 5.2 %multiply_reduce_fusion.5 = bf16[512,512]{1,0:T(8,128)(2,1)S(1)} fusion(bf16[4,512,512]{2,1,0:T(8,128)(2,1)} %get-tuple-element.272, f32[4]{0:T(128)S(1)} %dynamic-slice_bitcast_fusion.2, bf16[4,512,512]{2,1,0:T(8,128)(2,1)} %get-tuple-element.270, f32[512,512]{1,0:T(8,128)} %multiply_reduce_fusion.4, bf16[6,512,512]{2,1,0:T(8,128)(2,1)} %get-tuple-element.271, ...), kind=kOutput, calls=%fused_computation.clone.1 | convolution fusion | flops 2151153664 | bytes 6291476 | tf_op jit(solution)/shard_map/while/body/eval_jaxpr/kji,kjl->kil/dot_general | solution.py:100
  207.4 7.8 %dynamic_update_slice.4 = f32[6,1024,1024]{2,1,0:T(8,128)} dynamic-update-slice(f32[6,1024,1024]{2,1,0:T(8,128)} %get-tuple-element.248, f32[1,512,512]{2,1,0:T(8,128)S(1)} %copy.25, s32[]{:T(128)S(6)} %select_n.18, s32[]{:T(128)S(6)} %select_n.19, s32[]{:T(128)S(6)} %select_n.20) | dynamic-update-slice | bytes 2097156 | tf_op jit(solution)/shard_map/while/body/eval_jaxpr/dynamic_update_slice | solution.py:105
  236.3 5.2 %multiply_reduce_fusion.5 = bf16[512,512]{1,0:T(8,128)(2,1)S(1)} fusion(bf16[4,512,512]{2,1,0:T(8,128)(2,1)} %get-tuple-element.272, f32[4]{0:T(128)S(1)} %dynamic-slice_bitcast_fusion.2, bf16[4,512,512]{2,1,0:T(8,128)(2,1)} %get-tuple-element.270, f32[512,512]{1,0:T(8,128)} %multiply_reduce_fusion.4, bf16[6,512,512]{2,1,0:T(8,128)(2,1)} %get-tuple-element.271, ...), kind=kOutput, calls=%fused_computation.clone.1 | convolution fusion | flops 2151153664 | bytes 6291476 | tf_op jit(solution)/shard_map/while/body/eval_jaxpr/kji,kjl->kil/dot_general | solution.py:100
  242.0 7.5 %dynamic_update_slice.4 = f32[6,1024,1024]{2,1,0:T(8,128)} dynamic-update-slice(f32[6,1024,1024]{2,1,0:T(8,128)} %get-tuple-element.248, f32[1,512,512]{2,1,0:T(8,128)S(1)} %copy.25, s32[]{:T(128)S(6)} %select_n.18, s32[]{:T(128)S(6)} %select_n.19, s32[]{:T(128)S(6)} %select_n.20) | dynamic-update-slice | bytes 2097156 | tf_op jit(solution)/shard_map/while/body/eval_jaxpr/dynamic_update_slice | solution.py:105
  270.7 5.2 %multiply_reduce_fusion.5 = bf16[512,512]{1,0:T(8,128)(2,1)S(1)} fusion(bf16[4,512,512]{2,1,0:T(8,128)(2,1)} %get-tuple-element.272, f32[4]{0:T(128)S(1)} %dynamic-slice_bitcast_fusion.2, bf16[4,512,512]{2,1,0:T(8,128)(2,1)} %get-tuple-element.270, f32[512,512]{1,0:T(8,128)} %multiply_reduce_fusion.4, bf16[6,512,512]{2,1,0:T(8,128)(2,1)} %get-tuple-element.271, ...), kind=kOutput, calls=%fused_computation.clone.1 | convolution fusion | flops 2151153664 | bytes 6291476 | tf_op jit(solution)/shard_map/while/body/eval_jaxpr/kji,kjl->kil/dot_general | solution.py:100
  276.4 7.7 %dynamic_update_slice.4 = f32[6,1024,1024]{2,1,0:T(8,128)} dynamic-update-slice(f32[6,1024,1024]{2,1,0:T(8,128)} %get-tuple-element.248, f32[1,512,512]{2,1,0:T(8,128)S(1)} %copy.25, s32[]{:T(128)S(6)} %select_n.18, s32[]{:T(128)S(6)} %select_n.19, s32[]{:T(128)S(6)} %select_n.20) | dynamic-update-slice | bytes 2097156 | tf_op jit(solution)/shard_map/while/body/eval_jaxpr/dynamic_update_slice | solution.py:105
  305.3 5.2 %multiply_reduce_fusion.5 = bf16[512,512]{1,0:T(8,128)(2,1)S(1)} fusion(bf16[4,512,512]{2,1,0:T(8,128)(2,1)} %get-tuple-element.272, f32[4]{0:T(128)S(1)} %dynamic-slice_bitcast_fusion.2, bf16[4,512,512]{2,1,0:T(8,128)(2,1)} %get-tuple-element.270, f32[512,512]{1,0:T(8,128)} %multiply_reduce_fusion.4, bf16[6,512,512]{2,1,0:T(8,128)(2,1)} %get-tuple-element.271, ...), kind=kOutput, calls=%fused_computation.clone.1 | convolution fusion | flops 2151153664 | bytes 6291476 | tf_op jit(solution)/shard_map/while/body/eval_jaxpr/kji,kjl->kil/dot_general | solution.py:100
  310.9 7.8 %dynamic_update_slice.4 = f32[6,1024,1024]{2,1,0:T(8,128)} dynamic-update-slice(f32[6,1024,1024]{2,1,0:T(8,128)} %get-tuple-element.248, f32[1,512,512]{2,1,0:T(8,128)S(1)} %copy.25, s32[]{:T(128)S(6)} %select_n.18, s32[]{:T(128)S(6)} %select_n.19, s32[]{:T(128)S(6)} %select_n.20) | dynamic-update-slice | bytes 2097156 | tf_op jit(solution)/shard_map/while/body/eval_jaxpr/dynamic_update_slice | solution.py:105
  318.8 9.3 %convert.11 = bf16[6,1024,1024]{2,1,0:T(8,128)(2,1)S(1)} convert(f32[6,1024,1024]{2,1,0:T(8,128)} %get-tuple-element.110) | non-fusion elementwise | flops 6291456 | bytes 37748736 | tf_op jit(solution)/shard_map/convert.6
  335.4 12.2 %slice.152 = f32[6,1024,512]{2,1,0:T(8,128)} slice(f32[6,1024,1024]{2,1,0:T(8,128)} %get-tuple-element.110), slice={[0:6], [0:1024], [256:768]} | slice | bytes 25165824 | tf_op jit(solution)/shard_map/slice | solution.py:31
  347.5 19.9 %collective-permute-done.4 = bf16[6,1024,256]{2,1,0:T(8,128)(2,1)} collective-permute-done((bf16[6,1024,256]{2,1,0:T(8,128)(2,1)S(1)}, bf16[6,1024,256]{2,1,0:T(8,128)(2,1)}, u32[]{:S(2)}, u32[]{:S(2)}) %collective-permute-start.4) | collective-permute-done | bytes 3145760 | tf_op jit(solution)/shard_map/ppermute | solution.py:12
  367.4 7.3 %add_dynamic-update-slice_fusion = f32[6,1024,512]{2,1,0:T(8,128)} fusion(f32[6,1024,512]{2,1,0:T(8,128)} %slice.152, bf16[6,1024,256]{2,1,0:T(8,128)(2,1)} %collective-permute-done.4, f32[6,1024,1024]{2,1,0:T(8,128)} %get-tuple-element.110), kind=kLoop, calls=%fused_computation.22 | loop fusion | flops 3145728 | bytes 15728640 | tf_op jit(solution)/shard_map/scatter-add | solution.py:40
  374.7 7.3 %fusion.17 = f32[6,1024,512]{2,1,0:T(8,128)} fusion(f32[6,1024,512]{2,1,0:T(8,128)} %add_dynamic-update-slice_fusion, bf16[6,1024,256]{2,1,0:T(8,128)(2,1)} %collective-permute-done.5), kind=kLoop, calls=%fused_computation.19 | loop fusion | flops 3145728 | bytes 15728640 | tf_op jit(solution)/shard_map/scatter-add | solution.py:41
  382.0 5.4 %convert.12 = bf16[6,1024,512]{2,1,0:T(8,128)(2,1)S(1)} convert(f32[6,1024,512]{2,1,0:T(8,128)} %fusion.17) | non-fusion elementwise | flops 3145728 | bytes 18874368 | tf_op jit(solution)/shard_map/convert.4
  397.2 28.8 %collective-permute-done.6 = bf16[6,256,512]{2,1,0:T(8,128)(2,1)S(1)} collective-permute-done((bf16[6,256,512]{2,1,0:T(8,128)(2,1)S(1)}, bf16[6,256,512]{2,1,0:T(8,128)(2,1)S(1)}, u32[]{:S(2)}, u32[]{:S(2)}) %collective-permute-start.6) | collective-permute-done | bytes 1572896 | tf_op jit(solution)/shard_map/ppermute | solution.py:12
  (109 shorter events, 145.4 us)
Async XLA Ops:
  3.4 38.0 %collective-permute-start = (bf16[6,256,512]{2,1,0:T(8,128)(2,1)S(1)}, bf16[6,256,512]{2,1,0:T(8,128)(2,1)S(1)}, u32[]{:S(2)}, u32[]{:S(2)}) collective-permute-start(bf16[6,256,512]{2,1,0:T(8,128)(2,1)S(1)} %get-tuple-element.161), channel_id=1, source_target_pairs={{0,32},{32,64},{64,96},{1,33},{33,65},{65,97},{2,34},{34,66},{66,9... | collective-permute-start | bytes 4718600 | tf_op jit(solution)/shard_map/ppermute | solution.py:20
  6.9 37.7 %collective-permute-start.1 = (bf16[6,256,512]{2,1,0:T(8,128)(2,1)S(1)}, bf16[6,256,512]{2,1,0:T(8,128)(2,1)S(1)}, u32[]{:S(2)}, u32[]{:S(2)}) collective-permute-start(bf16[6,256,512]{2,1,0:T(8,128)(2,1)S(1)} %get-tuple-element.162), channel_id=1, source_target_pairs={{32,0},{64,32},{96,64},{33,1},{65,33},{97,65},{34,2},{66,34},{98,6... | collective-permute-start | bytes 4718600 | tf_op jit(solution)/shard_map/ppermute | solution.py:23
  41.4 3.2 copy-start
  44.6 1.1 copy-start.1
  46.2 9.0 %copy-start.2 = (f32[6,4]{0,1:T(4,128)S(1)}, f32[6,4]{0,1:T(4,128)}, u32[]{:S(2)}) copy-start(f32[6,4]{0,1:T(4,128)} %param.26) | copy-start | bytes 292
  46.3 9.1 %copy-start.3 = (s32[6,2]{0,1:T(2,128)S(1)}, s32[6,2]{0,1:T(2,128)}, u32[]{:S(2)}) copy-start(s32[6,2]{0,1:T(2,128)} %param.23) | copy-start | bytes 148
  46.3 9.0 %copy-start.4 = (s32[6,2]{0,1:T(2,128)S(1)}, s32[6,2]{0,1:T(2,128)}, u32[]{:S(2)}) copy-start(s32[6,2]{0,1:T(2,128)} %param.21) | copy-start | bytes 148
  49.6 38.9 %collective-permute-start.2 = (bf16[6,1024,256]{2,1,0:T(8,128)(2,1)}, bf16[6,1024,256]{2,1,0:T(8,128)(2,1)}, u32[]{:S(2)}, u32[]{:S(2)}) collective-permute-start(bf16[6,1024,256]{2,1,0:T(8,128)(2,1)} %get-tuple-element.159), channel_id=1, source_target_pairs={{0,1},{1,2},{2,3},{3,4},{4,5},{5,6},{6,7},{7,8},{8,9},{9,10},{10,1... | collective-permute-start | bytes 9437192 | tf_op jit(solution)/shard_map/ppermute | solution.py:20
  51.5 38.7 %collective-permute-start.3 = (bf16[6,1024,256]{2,1,0:T(8,128)(2,1)}, bf16[6,1024,256]{2,1,0:T(8,128)(2,1)}, u32[]{:S(2)}, u32[]{:S(2)}) collective-permute-start(bf16[6,1024,256]{2,1,0:T(8,128)(2,1)} %get-tuple-element.160), channel_id=1, source_target_pairs={{1,0},{2,1},{3,2},{4,3},{5,4},{6,5},{7,6},{8,7},{9,8},{10,9},{11,1... | collective-permute-start | bytes 9437192 | tf_op jit(solution)/shard_map/ppermute | solution.py:23
  99.9 11.5 %copy-start.6 = (s32[6]{0:T(128)S(1)}, s32[6]{0:T(128)}, u32[]{:S(2)}) copy-start(s32[6]{0:T(128)} %param.22) | copy-start | bytes 76
  328.7 38.7 %collective-permute-start.4 = (bf16[6,1024,256]{2,1,0:T(8,128)(2,1)S(1)}, bf16[6,1024,256]{2,1,0:T(8,128)(2,1)}, u32[]{:S(2)}, u32[]{:S(2)}) collective-permute-start(bf16[6,1024,256]{2,1,0:T(8,128)(2,1)S(1)} %get-tuple-element.156), channel_id=1, source_target_pairs={{0,1},{1,2},{2,3},{3,4},{4,5},{5,6},{6,7},{7,8},{8,9},{9,10},{10,1... | collective-permute-start | bytes 9437192 | tf_op jit(solution)/shard_map/ppermute | solution.py:12
  333.2 41.4 %collective-permute-start.5 = (bf16[6,1024,256]{2,1,0:T(8,128)(2,1)S(1)}, bf16[6,1024,256]{2,1,0:T(8,128)(2,1)}, u32[]{:S(2)}, u32[]{:S(2)}) collective-permute-start(bf16[6,1024,256]{2,1,0:T(8,128)(2,1)S(1)} %get-tuple-element.155), channel_id=1, source_target_pairs={{1,0},{2,1},{3,2},{4,3},{5,4},{6,5},{7,6},{8,7},{9,8},{10,9},{11,1... | collective-permute-start | bytes 9437192 | tf_op jit(solution)/shard_map/ppermute | solution.py:12
  387.7 38.2 %collective-permute-start.6 = (bf16[6,256,512]{2,1,0:T(8,128)(2,1)S(1)}, bf16[6,256,512]{2,1,0:T(8,128)(2,1)S(1)}, u32[]{:S(2)}, u32[]{:S(2)}) collective-permute-start(bf16[6,256,512]{2,1,0:T(8,128)(2,1)S(1)} %get-tuple-element.158), channel_id=1, source_target_pairs={{0,32},{32,64},{64,96},{1,33},{33,65},{65,97},{2,34},{34,66},{66,9... | collective-permute-start | bytes 4718600 | tf_op jit(solution)/shard_map/ppermute | solution.py:12
  390.8 37.7 %collective-permute-start.7 = (bf16[6,256,512]{2,1,0:T(8,128)(2,1)S(1)}, bf16[6,256,512]{2,1,0:T(8,128)(2,1)S(1)}, u32[]{:S(2)}, u32[]{:S(2)}) collective-permute-start(bf16[6,256,512]{2,1,0:T(8,128)(2,1)S(1)} %get-tuple-element.157), channel_id=1, source_target_pairs={{32,0},{64,32},{96,64},{33,1},{65,33},{97,65},{34,2},{66,34},{98,6... | collective-permute-start | bytes 4718600 | tf_op jit(solution)/shard_map/ppermute | solution.py:12
  425.9 3.4 slice-start
  428.5 1.7 slice-start.1
  428.5 1.7 copy-start.5
where the time goes:
time: 438 us; the launch traced here: 435 us
  local copies, waits for them, and re-layouts  122 us (28%)
  waiting for transfers between devices  119 us (27%)
  matrix products  83.1 us (19%)
  other arithmetic  51.1 us (12%)
  loops' own time  35.3 us (8%)
  starting transfers between devices  24.1 us (6%)
    ppermute x2, waiting for transfers between devices, extended_2(): lax.ppermute(lax.slice_in_dim(block, block.shape[dim] - width, None, axis...  65.3 us
    ppermute x4, waiting for transfers between devices, from_behind(): return lax.ppermute(value, axis, pairs)  48.6 us
    dynamic_update_slice x12, local copies, waits for them, and re-layouts, visit_segment(): lax.dynamic_update_slice(canvas_sum, current + adjoint.astype(jnp.float32...  48.2 us
    another operation x1, loops' own time, per_device(): lax.scan(visit_segment, empty_sum, (observed, psf_weights, segment_band,...  35.3 us
    dot_general x6, matrix products, visit_segment(): jnp.einsum('kji,kjl->kil', psf_rows, right_terms, preferred_element_type=...  30.9 us
    dot_general x6, matrix products, visit_segment(): jnp.dot(rows_flat, window, preferred_element_type=jnp.float32)  28.7 us
    dot_general x6, matrix products, visit_segment(): jnp.einsum('kij,klj->kil', left_terms, psf_cols, preferred_element_type=j...  23.5 us
    reshape x6, local copies, waits for them, and re-layouts, visit_segment(): left_terms = left_terms.reshape(term_count, pixels, pixels)  17.2 us
  transfers between devices with their start and end apart: 8, of which 6 were waited for; matrix products, arithmetic and copies ran while one was open for 6% of the time, Pallas kernels for 0%

commit v1 on v0

v1 whole, which is shorter than its diff:
```python
import functools

import jax
import jax.numpy as jnp
from jax import lax
from jax.experimental import pallas as pl
from jax.experimental.pallas import tpu as pltpu
from jax.sharding import PartitionSpec as P

TILE = 128


def shift(value, axis, by):
    count = lax.axis_size(axis)
    pairs = [(i, i + by) for i in range(count) if 0 <= i + by < count]
    return lax.ppermute(value, axis, pairs)


def halo(block, rim):
    side = block.shape[1]
    up = shift(block[:, side - rim :, :], "sky", 1)
    down = shift(block[:, :rim, :], "sky", -1)
    left = shift(block[:, :, side - rim :], "visit", 1)
    right = shift(block[:, :, :rim], "visit", -1)
    from_left = shift(
        jnp.concatenate([up[:, :, side - rim :], down[:, :, side - rim :]], axis=1), "visit", 1
    )
    from_right = shift(jnp.concatenate([up[:, :, :rim], down[:, :, :rim]], axis=1), "visit", -1)
    top = jnp.concatenate([from_left[:, :rim], up, from_right[:, :rim]], axis=2)
    middle = jnp.concatenate([left, block, right], axis=2)
    bottom = jnp.concatenate([from_left[:, rim:], down, from_right[:, rim:]], axis=2)
    return jnp.concatenate([top, middle, bottom], axis=1)


def fold(canvas, rim):
    full = canvas.shape[1]
    side = full - 2 * rim
    bf = jnp.bfloat16
    lo, hi = slice(0, rim), slice(full - rim, full)
    mid = slice(rim, rim + side)
    to_left = jnp.concatenate([canvas[:, lo, lo], canvas[:, hi, lo]], axis=1).astype(bf)
    to_right = jnp.concatenate([canvas[:, lo, hi], canvas[:, hi, hi]], axis=1).astype(bf)
    got_right = shift(to_left, "visit", -1).astype(jnp.float32)
    got_left = shift(to_right, "visit", 1).astype(jnp.float32)
    top = canvas[:, lo, mid]
    bottom = canvas[:, hi, mid]
    top = top + jnp.concatenate([got_left[:, :rim], got_right[:, :rim]], axis=2)
    bottom = bottom + jnp.concatenate([got_left[:, rim:], got_right[:, rim:]], axis=2)
    from_down = shift(top.astype(bf), "sky", -1).astype(jnp.float32)
    from_up = shift(bottom.astype(bf), "sky", 1).astype(jnp.float32)
    from_right = shift(canvas[:, mid, lo].astype(bf), "visit", -1).astype(jnp.float32)
    from_left = shift(canvas[:, mid, hi].astype(bf), "visit", 1).astype(jnp.float32)
    interior = canvas[:, mid, mid]
    interior = interior.at[:, :rim, :].add(from_up)
    interior = interior.at[:, side - rim :, :].add(from_down)
    interior = interior.at[:, :, :rim].add(from_left)
    interior = interior.at[:, :, side - rim :].add(from_right)
    return interior


def segment_kernel(terms, w_ref, win_ref, obs_ref, rows_ref, rows_t_ref, cols_ref, cols_t_ref,
                   out_ref, acc_ref, res_ref):
    seg = pl.program_id(0)
    f32 = jnp.float32
    acc_ref[...] = jnp.zeros(acc_ref.shape, f32)

    def forward(k, carry):
        left = jnp.dot(rows_ref[k], win_ref[0], preferred_element_type=f32).astype(jnp.bfloat16)
        acc_ref[...] += w_ref[seg, k] * jnp.dot(left, cols_t_ref[k], preferred_element_type=f32)
        return carry

    lax.fori_loop(0, terms, forward, 0)
    res_ref[...] = (acc_ref[...] - obs_ref[0].astype(f32)).astype(jnp.bfloat16)
    acc_ref[...] = jnp.zeros(acc_ref.shape, f32)

    def backward(k, carry):
        right = jnp.dot(res_ref[...], cols_ref[k], preferred_element_type=f32).astype(jnp.bfloat16)
        acc_ref[...] += w_ref[seg, k] * jnp.dot(rows_t_ref[k], right, preferred_element_type=f32)
        return carry

    lax.fori_loop(0, terms, backward, 0)
    out_ref[0] = acc_ref[...].astype(out_ref.dtype)


def adjoints(windows, observed, psf_rows, psf_cols, psf_weights):
    segs, pix, _ = windows.shape
    terms = psf_rows.shape[0]
    rows_t = jnp.swapaxes(psf_rows, 1, 2)
    cols_t = jnp.swapaxes(psf_cols, 1, 2)
    seg_spec = pl.BlockSpec((1, pix, pix), lambda i: (i, 0, 0))
    psf_spec = pl.BlockSpec((terms, pix, pix), lambda i: (0, 0, 0))
    flops = segs * terms * 4 * 2 * pix ** 3
    moved = 2 * pix * pix * (3 * segs + 4 * terms)
    return pl.pallas_call(
        functools.partial(segment_kernel, terms),
        grid=(segs,),
        in_specs=[
            pl.BlockSpec(memory_space=pltpu.SMEM),
            seg_spec,
            seg_spec,
            psf_spec,
            psf_spec,
            psf_spec,
            psf_spec,
        ],
        out_specs=seg_spec,
        out_shape=jax.ShapeDtypeStruct((segs, pix, pix), jnp.bfloat16),
        scratch_shapes=[
            pltpu.VMEM((pix, pix), jnp.float32),
            pltpu.VMEM((pix, pix), jnp.bfloat16),
        ],
        compiler_params=pltpu.CompilerParams(
            dimension_semantics=("arbitrary",), vmem_limit_bytes=56 * 1024 * 1024
        ),
        cost_estimate=pl.CostEstimate(flops=flops, bytes_accessed=moved, transcendentals=0),
    )(psf_weights, windows, observed, psf_rows, rows_t, psf_cols, cols_t)


def per_device(
    sky_image,
    observed,
    footprint,
    segment_band,
    offsets,
    psf_rows,
    psf_cols,
    psf_weights,
    step_sizes,
):
    block_side = sky_image.shape[1]
    pixels = observed.shape[1]
    segs = observed.shape[0]
    rim = (pixels // TILE + 1) // 2 * TILE
    sky_bf = sky_image.astype(jnp.bfloat16)
    extended = halo(sky_bf, rim)
    row_anchor = lax.axis_index("sky") * block_side - rim
    col_anchor = lax.axis_index("visit") * block_side - rim
    top_rows = footprint[:, 0] * TILE + offsets[:, 0] - row_anchor
    left_cols = footprint[:, 1] * TILE + offsets[:, 1] - col_anchor
    windows = jnp.stack(
        [
            lax.dynamic_slice(
                extended, (segment_band[s], top_rows[s], left_cols[s]), (1, pixels, pixels)
            )[0]
            for s in range(segs)
        ]
    )
    adj = adjoints(windows, observed, psf_rows, psf_cols, psf_weights)
    canvas = jnp.zeros(extended.shape, jnp.float32)
    for s in range(segs):
        at = (segment_band[s], top_rows[s], left_cols[s])
        current = lax.dynamic_slice(canvas, at, (1, pixels, pixels))
        canvas = lax.dynamic_update_slice(
            canvas, current + adj[s].astype(jnp.float32)[None], at
        )
    gradient = fold(canvas, rim)
    return sky_image - step_sizes[:, None, None] * gradient


def solution(mesh):
    placed = (
        P(None, "sky", "visit"),
        P(("sky", "visit"), None, None),
        P(("sky", "visit"), None),
        P(("sky", "visit")),
        P(("sky", "visit"), None),
        P(),
        P(),
        P(("sky", "visit"), None),
        P(),
    )
    return jax.shard_map(
        per_device, mesh=mesh, in_specs=placed, out_specs=P(None, "sky", "visit"), check_vma=False
    )
```

time: 438 us -> 331 us (0.76)
  matrix products: 83.1 us -> 0 us
  Pallas kernels: 0 us -> 42.1 us
  waiting for transfers between devices: 119 us -> 77.6 us
  local copies, waits for them, and re-layouts: 122 us -> 85.9 us
  loops' own time: 35.3 us -> 0 us
  between operations: 0.22 us -> 35.1 us
  starting transfers between devices: 24.1 us -> 33.8 us
    dot_general x18 -> x0, matrix products: 83.1 us -> none  [the longest x6 30.9 us: visit_segment(): jnp.einsum('kji,kjl->kil', psf_rows, right_terms, preferred_element_type=...]
    pallas_call x0 -> x1, Pallas kernels: none -> 42.1 us  [adjoints(): pl.pallas_call(functools.partial(segment_kernel, terms), grid=(segs,), in...]
    ppermute x8 -> x12, waiting for transfers between devices: 119 us -> 77.6 us  [shift(): return lax.ppermute(value, axis, pairs)]
    another operation x1 -> x0, loops' own time: 35.3 us -> none  [per_device(): lax.scan(visit_segment, empty_sum, (observed, psf_weights, segment_band,...]
    dynamic_slice x30 -> x0, local copies, waits for them, and re-layouts: 22.6 us -> none  [the longest x12 12.1 us: visit_segment(): lax.dynamic_slice(canvas_sum, (band_index, top, left_col), (1, pixels, pi...]
    reshape x6 -> x0, local copies, waits for them, and re-layouts: 17.2 us -> none  [visit_segment(): left_terms = left_terms.reshape(term_count, pixels, pixels)]
    unnamed x18 -> x44, local copies, waits for them, and re-layouts: 2.11 us -> 13.3 us
    ppermute x8 -> x12, starting transfers between devices: 24.1 us -> 33.8 us  [shift(): return lax.ppermute(value, axis, pairs)]
  transfers between devices with their start and end apart: 8 -> 12, of which waited for: 6 -> 6; matrix products, arithmetic and copies ran while one was open for 6% -> 9% of each run, Pallas kernels for 0% -> 0%
where the time goes in v1:
time: 331 us; the launch traced here: 326 us
  local copies, waits for them, and re-layouts  85.9 us (26%)
  waiting for transfers between devices  77.6 us (23%)
  other arithmetic  51.5 us (16%)
  Pallas kernels  42.1 us (13%)
  between operations  35.1 us (11%)
  starting transfers between devices  33.8 us (10%)
    ppermute x12, waiting for transfers between devices, shift(): return lax.ppermute(value, axis, pairs)  77.6 us
    dynamic_update_slice x6, local copies, waits for them, and re-layouts, per_device(): lax.dynamic_update_slice(canvas, current + adj[s].astype(jnp.float32)[Non...  45.8 us
    pallas_call x1, Pallas kernels, adjoints(): pl.pallas_call(functools.partial(segment_kernel, terms), grid=(segs,), in...  42.1 us
    ppermute x12, starting transfers between devices, shift(): return lax.ppermute(value, axis, pairs)  33.8 us
    another operation x1, other arithmetic  15.8 us
    unnamed x44, local copies, waits for them, and re-layouts  13.3 us
    broadcast_in_dim x1, local copies, waits for them, and re-layouts, per_device(): canvas = jnp.zeros(extended.shape, jnp.float32)  11.5 us
    add x5, other arithmetic, per_device(): current + adj[s].astype(jnp.float32)[None]  8.91 us
  transfers between devices with their start and end apart: 12, of which 6 were waited for; matrix products, arithmetic and copies ran while one was open for 9% of the time, Pallas kernels for 0%

profile of v1, /device:TPU:104, one launch (start us, length us, event | category | flops | bytes accessed | tf_op | source)
XLA Modules:
  0.0 325.9 jit_solution(14032010309939431928)
XLA Ops:
  0.0 3.2 convert_element_type.55
  3.4 3.5 %collective-permute-start = (bf16[6,256,512]{2,1,0:T(8,128)(2,1)S(1)}, bf16[6,256,512]{2,1,0:T(8,128)(2,1)S(1)}, u32[]{:S(2)}, u32[]{:S(2)}) collective-permute-start(bf16[6,256,512]{2,1,0:T(8,128)(2,1)S(1)} %get-tuple-element.63), channel_id=1, source_target_pairs={{0,32},{32,64},{64,96},{1,33},{33,65},{65,97},{2,34},{34,66},{66,9... | collective-permute-start | bytes 4718600 | tf_op jit(solution)/shard_map/ppermute | solution.py:16
  9.4 32.1 %collective-permute-done = bf16[6,256,512]{2,1,0:T(8,128)(2,1)S(1)} collective-permute-done((bf16[6,256,512]{2,1,0:T(8,128)(2,1)S(1)}, bf16[6,256,512]{2,1,0:T(8,128)(2,1)S(1)}, u32[]{:S(2)}, u32[]{:S(2)}) %collective-permute-start) | collective-permute-done | bytes 1572896 | tf_op jit(solution)/shard_map/ppermute | solution.py:16
  41.6 3.1 collective-permute-done.1
  54.8 3.9 %collective-permute-start.4 = (bf16[6,512,256]{2,1,0:T(8,128)(2,1)}, bf16[6,512,256]{2,1,0:T(8,128)(2,1)}, u32[]{:S(2)}, u32[]{:S(2)}) collective-permute-start(bf16[6,512,256]{2,1,0:T(8,128)(2,1)} %get-tuple-element.61), channel_id=1, source_target_pairs={{0,1},{1,2},{2,3},{3,4},{4,5},{5,6},{6,7},{7,8},{8,9},{9,10},{10,1... | collective-permute-start | bytes 4718600 | tf_op jit(solution)/shard_map/ppermute | solution.py:16
  86.1 4.1 %copy.10 = bf16[4,512,512]{1,2,0:T(8,128)(2,1)} copy(bf16[4,512,512]{2,1,0:T(8,128)(2,1)} %rows_ref.1) | data formatting | bytes 4194304 | tf_op args[5]
  90.2 4.1 %copy.11 = bf16[4,512,512]{1,2,0:T(8,128)(2,1)} copy(bf16[4,512,512]{2,1,0:T(8,128)(2,1)} %cols_ref.1) | data formatting | bytes 4194304 | tf_op args[6]
  109.0 4.4 %maximum_maximum_fusion = bf16[6,1024,1024]{2,1,0:T(8,128)(2,1)S(1)} fusion(bf16[6,256,256]{2,1,0:T(8,128)(2,1)S(1)} %get-tuple-element.72, bf16[6,256,512]{2,1,0:T(8,128)(2,1)S(1)} %copy-done.3, bf16[6,256,256]{2,1,0:T(8,128)(2,1)S(1)} %get-tuple-element.70, bf16[6,512,256]{2,1,0:T(8,128)(2,1)} %collective-permute-done.5, ...), kind=kLoop, calls=%fused_computation | loop fusion | flops 113246208 | bytes 25165824 | tf_op jit(solution)/shard_map/concatenate | solution.py:32
  117.0 42.1 %shard_map.91 = bf16[6,512,512]{2,1,0:T(8,128)(2,1)} custom-call(f32[6,4]{1,0:T(8,128)} %copy.12.w_ref, bf16[6,512,512]{2,1,0:T(8,128)(2,1)} %copy-done.4, bf16[6,512,512]{2,1,0:T(8,128)(2,1)} %obs_ref.1, bf16[4,512,512]{2,1,0:T(8,128)(2,1)} %rows_ref.1, bf16[4,512,512]{2,1,0:T(8,128)(2,1)} %bitcast.24, bf16[4,512,512]{2,1,0:T(8,128)(2,1)} %cols_ref.1, ...), custom_call_target="tpu_custom_call" | custom-call | flops 25769803776 | bytes 17825792 | tf_op jit(solution)/shard_map/pallas_call | solution.py:94
  160.3 11.5 %broadcast_in_dim.2 = f32[6,1024,1024]{2,1,0:T(8,128)} broadcast(f32[]{:T(128)} %constant.119.clone.1), dimensions={} | broadcast | bytes 25165828 | tf_op jit(solution)/shard_map/broadcast_in_dim | solution.py:149
  171.8 7.7 %dynamic_update_slice.18 = f32[6,1024,1024]{2,1,0:T(8,128)} dynamic-update-slice(f32[6,1024,1024]{2,1,0:T(8,128)} %broadcast_in_dim.2, f32[1,512,512]{2,1,0:T(8,128)S(1)} %slice_convert_fusion, s32[]{:T(128)S(6)} %select_n.36, s32[]{:T(128)S(6)} %select_n.37, s32[]{:T(128)S(6)} %select_n.38) | dynamic-update-slice | bytes 2097156 | tf_op jit(solution)/shard_map/dynamic_update_slice | solution.py:153
  181.3 7.8 %dynamic_update_slice.19 = f32[6,1024,1024]{2,1,0:T(8,128)} dynamic-update-slice(f32[6,1024,1024]{2,1,0:T(8,128)} %dynamic_update_slice.18, f32[1,512,512]{2,1,0:T(8,128)S(1)} %convert_add_fusion.4, s32[]{:T(128)S(6)} %select_n.39, s32[]{:T(128)S(6)} %select_n.40, s32[]{:T(128)S(6)} %select_n.41) | dynamic-update-slice | bytes 2097156 | tf_op jit(solution)/shard_map/dynamic_update_slice | solution.py:153
  191.0 7.5 %dynamic_update_slice.20 = f32[6,1024,1024]{2,1,0:T(8,128)} dynamic-update-slice(f32[6,1024,1024]{2,1,0:T(8,128)} %dynamic_update_slice.19, f32[1,512,512]{2,1,0:T(8,128)S(1)} %convert_add_fusion.3, s32[]{:T(128)S(6)} %select_n.42, s32[]{:T(128)S(6)} %select_n.43, s32[]{:T(128)S(6)} %select_n.44) | dynamic-update-slice | bytes 2097156 | tf_op jit(solution)/shard_map/dynamic_update_slice | solution.py:153
  200.3 7.7 %dynamic_update_slice.21 = f32[6,1024,1024]{2,1,0:T(8,128)} dynamic-update-slice(f32[6,1024,1024]{2,1,0:T(8,128)} %dynamic_update_slice.20, f32[1,512,512]{2,1,0:T(8,128)S(1)} %convert_add_fusion.2, s32[]{:T(128)S(6)} %select_n.45, s32[]{:T(128)S(6)} %select_n.46, s32[]{:T(128)S(6)} %select_n.47) | dynamic-update-slice | bytes 2097156 | tf_op jit(solution)/shard_map/dynamic_update_slice | solution.py:153
  209.7 7.5 %dynamic_update_slice.22 = f32[6,1024,1024]{2,1,0:T(8,128)} dynamic-update-slice(f32[6,1024,1024]{2,1,0:T(8,128)} %dynamic_update_slice.21, f32[1,512,512]{2,1,0:T(8,128)S(1)} %convert_add_fusion.1, s32[]{:T(128)S(6)} %select_n.48, s32[]{:T(128)S(6)} %select_n.49, s32[]{:T(128)S(6)} %select_n.50) | dynamic-update-slice | bytes 2097156 | tf_op jit(solution)/shard_map/dynamic_update_slice | solution.py:153
  219.1 7.5 %dynamic_update_slice.23 = f32[6,1024,1024]{2,1,0:T(8,128)} dynamic-update-slice(f32[6,1024,1024]{2,1,0:T(8,128)} %dynamic_update_slice.22, f32[1,512,512]{2,1,0:T(8,128)S(1)} %convert_add_fusion, s32[]{:T(128)S(6)} %select_n.102, s32[]{:T(128)S(6)} %select_n.103, s32[]{:T(128)S(6)} %select_n.104) | dynamic-update-slice | bytes 2097156 | tf_op jit(solution)/shard_map/dynamic_update_slice | solution.py:153
  226.6 15.8 %convert.12 = bf16[6,1024,1024]{2,1,0:T(8,128)(2,1)} convert(f32[6,1024,1024]{2,1,0:T(8,128)} %dynamic_update_slice.23) | non-fusion elementwise | flops 6291456 | bytes 37748736 | tf_op jit(solution)/shard_map/convert.9
  250.3 15.0 %collective-permute-done.7 = bf16[6,512,256]{2,1,0:T(8,128)(2,1)S(1)} collective-permute-done((bf16[6,512,256]{2,1,0:T(8,128)(2,1)S(1)}, bf16[6,512,256]{2,1,0:T(8,128)(2,1)S(1)}, u32[]{:S(2)}, u32[]{:S(2)}) %collective-permute-start.7) | collective-permute-done | bytes 1572896 | tf_op jit(solution)/shard_map/ppermute | solution.py:16
  265.6 3.9 %collective-permute-done.6 = bf16[6,512,256]{2,1,0:T(8,128)(2,1)S(1)} collective-permute-done((bf16[6,512,256]{2,1,0:T(8,128)(2,1)S(1)}, bf16[6,512,256]{2,1,0:T(8,128)(2,1)S(1)}, u32[]{:S(2)}, u32[]{:S(2)}) %collective-permute-start.6) | collective-permute-done | bytes 1572896 | tf_op jit(solution)/shard_map/ppermute | solution.py:16
  272.0 3.4 %collective-permute-start.8 = (bf16[6,256,512]{2,1,0:T(8,128)(2,1)}, bf16[6,256,512]{2,1,0:T(8,128)(2,1)}, u32[]{:S(2)}, u32[]{:S(2)}) collective-permute-start(bf16[6,256,512]{2,1,0:T(8,128)(2,1)} %get-tuple-element.54), channel_id=1, source_target_pairs={{0,32},{32,64},{64,96},{1,33},{33,65},{65,97},{2,34},{34,66},{66,9... | collective-permute-start | bytes 4718600 | tf_op jit(solution)/shard_map/ppermute | solution.py:16
  275.4 3.6 %collective-permute-start.9 = (bf16[6,256,512]{2,1,0:T(8,128)(2,1)}, bf16[6,256,512]{2,1,0:T(8,128)(2,1)}, u32[]{:S(2)}, u32[]{:S(2)}) collective-permute-start(bf16[6,256,512]{2,1,0:T(8,128)(2,1)} %get-tuple-element.53), channel_id=1, source_target_pairs={{32,0},{64,32},{96,64},{33,1},{65,33},{97,65},{34,2},{66,34},{98,6... | collective-permute-start | bytes 4718600 | tf_op jit(solution)/shard_map/ppermute | solution.py:16
  279.0 3.8 %fusion.6 = (bf16[6,512,256]{2,1,0:T(8,128)(2,1)}, bf16[6,512,256]{2,1,0:T(8,128)(2,1)}) fusion(bf16[6,1024,1024]{2,1,0:T(8,128)(2,1)} %convert.12), kind=kLoop, calls=%fused_computation.32 | loop fusion | bytes 6291456 | tf_op jit(solution)/shard_map/slice | solution.py:51
  289.1 21.7 %collective-permute-done.8 = bf16[6,256,512]{2,1,0:T(8,128)(2,1)} collective-permute-done((bf16[6,256,512]{2,1,0:T(8,128)(2,1)}, bf16[6,256,512]{2,1,0:T(8,128)(2,1)}, u32[]{:S(2)}, u32[]{:S(2)}) %collective-permute-start.8) | collective-permute-done | bytes 1572896 | tf_op jit(solution)/shard_map/ppermute | solution.py:16
  321.6 4.3 %multiply_subtract_fusion = f32[6,512,512]{2,1,0:T(8,128)} fusion(f32[6,512,512]{2,1,0:T(8,128)S(1)} %bitcast.23, f32[6,512,512]{2,1,0:T(8,128)S(1)} %fusion, f32[6]{0:T(128)S(1)} %copy-done.9), kind=kLoop, calls=%fused_computation.1 | loop fusion | flops 3145728 | bytes 18874392 | tf_op jit(solution)/shard_map/sub | solution.py:157
  (88 shorter events, 61.6 us)
Async XLA Ops:
  3.4 38.0 %collective-permute-start = (bf16[6,256,512]{2,1,0:T(8,128)(2,1)S(1)}, bf16[6,256,512]{2,1,0:T(8,128)(2,1)S(1)}, u32[]{:S(2)}, u32[]{:S(2)}) collective-permute-start(bf16[6,256,512]{2,1,0:T(8,128)(2,1)S(1)} %get-tuple-element.63), channel_id=1, source_target_pairs={{0,32},{32,64},{64,96},{1,33},{33,65},{65,97},{2,34},{34,66},{66,9... | collective-permute-start | bytes 4718600 | tf_op jit(solution)/shard_map/ppermute | solution.py:16
  6.9 37.7 %collective-permute-start.1 = (bf16[6,256,512]{2,1,0:T(8,128)(2,1)S(1)}, bf16[6,256,512]{2,1,0:T(8,128)(2,1)S(1)}, u32[]{:S(2)}, u32[]{:S(2)}) collective-permute-start(bf16[6,256,512]{2,1,0:T(8,128)(2,1)S(1)} %get-tuple-element.64), channel_id=1, source_target_pairs={{32,0},{64,32},{96,64},{33,1},{65,33},{97,65},{34,2},{66,34},{98,6... | collective-permute-start | bytes 4718600 | tf_op jit(solution)/shard_map/ppermute | solution.py:16
  41.4 3.4 %copy-start = (bf16[6,256,512]{2,1,0:T(8,128)(2,1)}, bf16[6,256,512]{2,1,0:T(8,128)(2,1)S(1)}, u32[]{:S(2)}) copy-start(bf16[6,256,512]{2,1,0:T(8,128)(2,1)S(1)} %collective-permute-done) | copy-start | bytes 4718596
  47.1 58.8 %collective-permute-start.3 = (bf16[6,512,256]{2,1,0:T(8,128)(2,1)}, bf16[6,512,256]{2,1,0:T(8,128)(2,1)}, u32[]{:S(2)}, u32[]{:S(2)}) collective-permute-start(bf16[6,512,256]{2,1,0:T(8,128)(2,1)} %pad_maximum_fusion.1), channel_id=1, source_target_pairs={{1,0},{2,1},{3,2},{4,3},{5,4},{6,5},{7,6},{8,7},{9,8},{10,9},{11,1... | collective-permute-start | bytes 4718600 | tf_op jit(solution)/shard_map/ppermute | solution.py:16
  50.3 10.6 %copy-start.5 = (s32[6]{0:T(128)S(1)}, s32[6]{0:T(128)}, u32[]{:S(2)}) copy-start(s32[6]{0:T(128)} %param.20) | copy-start | bytes 76
  50.3 19.1 %copy-start.7 = (s32[6,2]{0,1:T(2,128)S(1)}, s32[6,2]{0,1:T(2,128)}, u32[]{:S(2)}) copy-start(s32[6,2]{0,1:T(2,128)} %param.21) | copy-start | bytes 148
  50.3 19.1 %copy-start.8 = (s32[6,2]{0,1:T(2,128)S(1)}, s32[6,2]{0,1:T(2,128)}, u32[]{:S(2)}) copy-start(s32[6,2]{0,1:T(2,128)} %param.19) | copy-start | bytes 148
  50.3 35.1 %copy-start.6 = (f32[6,4]{0,1:T(4,128)S(1)}, f32[6,4]{0,1:T(4,128)}, u32[]{:S(2)}) copy-start(f32[6,4]{0,1:T(4,128)} %param.24) | copy-start | bytes 292
  50.3 57.2 %collective-permute-start.2 = (bf16[6,512,256]{2,1,0:T(8,128)(2,1)}, bf16[6,512,256]{2,1,0:T(8,128)(2,1)}, u32[]{:S(2)}, u32[]{:S(2)}) collective-permute-start(bf16[6,512,256]{2,1,0:T(8,128)(2,1)} %pad_maximum_fusion), channel_id=1, source_target_pairs={{0,1},{1,2},{2,3},{3,4},{4,5},{5,6},{6,7},{7,8},{8,9},{9,10},{10,1... | collective-permute-start | bytes 4718600 | tf_op jit(solution)/shard_map/ppermute | solution.py:16
  54.8 54.2 %collective-permute-start.4 = (bf16[6,512,256]{2,1,0:T(8,128)(2,1)}, bf16[6,512,256]{2,1,0:T(8,128)(2,1)}, u32[]{:S(2)}, u32[]{:S(2)}) collective-permute-start(bf16[6,512,256]{2,1,0:T(8,128)(2,1)} %get-tuple-element.61), channel_id=1, source_target_pairs={{0,1},{1,2},{2,3},{3,4},{4,5},{5,6},{6,7},{7,8},{8,9},{9,10},{10,1... | collective-permute-start | bytes 4718600 | tf_op jit(solution)/shard_map/ppermute | solution.py:16
  58.8 50.2 %collective-permute-start.5 = (bf16[6,512,256]{2,1,0:T(8,128)(2,1)}, bf16[6,512,256]{2,1,0:T(8,128)(2,1)}, u32[]{:S(2)}, u32[]{:S(2)}) collective-permute-start(bf16[6,512,256]{2,1,0:T(8,128)(2,1)} %get-tuple-element.62), channel_id=1, source_target_pairs={{1,0},{2,1},{3,2},{4,3},{5,4},{6,5},{7,6},{8,7},{9,8},{10,9},{11,1... | collective-permute-start | bytes 4718600 | tf_op jit(solution)/shard_map/ppermute | solution.py:16
  226.6 43.2 %slice-start = ((s8[25165824]{0:T(1024)(128)(4,1)}), s8[4194304]{0:T(1024)(128)(4,1)S(1)}, s32[]{:S(2)}) async-start(s8[25165824]{0:T(1024)(128)(4,1)} %bitcast.20), calls=%async_computation | async-start | bytes 8388608
  226.6 43.2 %slice-start.1 = ((s8[25165824]{0:T(1024)(128)(4,1)}), s8[4194304]{0:T(1024)(128)(4,1)S(1)}, s32[]{:S(2)}) async-start(s8[25165824]{0:T(1024)(128)(4,1)} %bitcast.20), calls=%async_computation.1 | async-start | bytes 8388608
  226.6 43.2 %slice-start.2 = ((s8[25165824]{0:T(1024)(128)(4,1)}), s8[4194304]{0:T(1024)(128)(4,1)S(1)}, s32[]{:S(2)}) async-start(s8[25165824]{0:T(1024)(128)(4,1)} %bitcast.20), calls=%async_computation.2 | async-start | bytes 8388608
  226.6 43.2 %slice-start.3 = ((s8[25165824]{0:T(1024)(128)(4,1)}), s8[4194304]{0:T(1024)(128)(4,1)S(1)}, s32[]{:S(2)}) async-start(s8[25165824]{0:T(1024)(128)(4,1)} %bitcast.20), calls=%async_computation.3 | async-start | bytes 8388608
  242.3 27.5 %slice-start.4 = ((s8[25165824]{0:T(1024)(128)(4,1)}), s8[4194304]{0:T(1024)(128)(4,1)S(1)}, s32[]{:S(2)}) async-start(s8[25165824]{0:T(1024)(128)(4,1)} %bitcast.20), calls=%async_computation.4 | async-start | bytes 8388608
  245.4 19.9 %collective-permute-start.7 = (bf16[6,512,256]{2,1,0:T(8,128)(2,1)S(1)}, bf16[6,512,256]{2,1,0:T(8,128)(2,1)S(1)}, u32[]{:S(2)}, u32[]{:S(2)}) collective-permute-start(bf16[6,512,256]{2,1,0:T(8,128)(2,1)S(1)} %pad_maximum_fusion.3), channel_id=1, source_target_pairs={{1,0},{2,1},{3,2},{4,3},{5,4},{6,5},{7,6},{8,7},{9,8},{10,9},{11,1... | collective-permute-start | bytes 4718600 | tf_op jit(solution)/shard_map/ppermute | solution.py:16
  247.5 22.3 %slice-start.5 = ((s8[25165824]{0:T(1024)(128)(4,1)}), s8[4194304]{0:T(1024)(128)(4,1)S(1)}, s32[]{:S(2)}) async-start(s8[25165824]{0:T(1024)(128)(4,1)} %bitcast.20), calls=%async_computation.5 | async-start | bytes 8388608
  247.5 22.0 %collective-permute-start.6 = (bf16[6,512,256]{2,1,0:T(8,128)(2,1)S(1)}, bf16[6,512,256]{2,1,0:T(8,128)(2,1)S(1)}, u32[]{:S(2)}, u32[]{:S(2)}) collective-permute-start(bf16[6,512,256]{2,1,0:T(8,128)(2,1)S(1)} %pad_maximum_fusion.2), channel_id=1, source_target_pairs={{0,1},{1,2},{2,3},{3,4},{4,5},{5,6},{6,7},{7,8},{8,9},{9,10},{10,1... | collective-permute-start | bytes 4718600 | tf_op jit(solution)/shard_map/ppermute | solution.py:16
  272.0 38.8 %collective-permute-start.8 = (bf16[6,256,512]{2,1,0:T(8,128)(2,1)}, bf16[6,256,512]{2,1,0:T(8,128)(2,1)}, u32[]{:S(2)}, u32[]{:S(2)}) collective-permute-start(bf16[6,256,512]{2,1,0:T(8,128)(2,1)} %get-tuple-element.54), channel_id=1, source_target_pairs={{0,32},{32,64},{64,96},{1,33},{33,65},{65,97},{2,34},{34,66},{66,9... | collective-permute-start | bytes 4718600 | tf_op jit(solution)/shard_map/ppermute | solution.py:16
  275.4 39.2 %collective-permute-start.9 = (bf16[6,256,512]{2,1,0:T(8,128)(2,1)}, bf16[6,256,512]{2,1,0:T(8,128)(2,1)}, u32[]{:S(2)}, u32[]{:S(2)}) collective-permute-start(bf16[6,256,512]{2,1,0:T(8,128)(2,1)} %get-tuple-element.53), channel_id=1, source_target_pairs={{32,0},{64,32},{96,64},{33,1},{65,33},{97,65},{34,2},{66,34},{98,6... | collective-permute-start | bytes 4718600 | tf_op jit(solution)/shard_map/ppermute | solution.py:16
  282.8 33.9 %collective-permute-start.10 = (bf16[6,512,256]{2,1,0:T(8,128)(2,1)}, bf16[6,512,256]{2,1,0:T(8,128)(2,1)}, u32[]{:S(2)}, u32[]{:S(2)}) collective-permute-start(bf16[6,512,256]{2,1,0:T(8,128)(2,1)} %get-tuple-element.56), channel_id=1, source_target_pairs={{0,1},{1,2},{2,3},{3,4},{4,5},{5,6},{6,7},{7,8},{8,9},{9,10},{10,1... | collective-permute-start | bytes 4718600 | tf_op jit(solution)/shard_map/ppermute | solution.py:16
  285.8 33.4 %collective-permute-start.11 = (bf16[6,512,256]{2,1,0:T(8,128)(2,1)}, bf16[6,512,256]{2,1,0:T(8,128)(2,1)}, u32[]{:S(2)}, u32[]{:S(2)}) collective-permute-start(bf16[6,512,256]{2,1,0:T(8,128)(2,1)} %get-tuple-element.55), channel_id=1, source_target_pairs={{1,0},{2,1},{3,2},{4,3},{5,4},{6,5},{7,6},{8,7},{9,8},{10,9},{11,1... | collective-permute-start | bytes 4718600 | tf_op jit(solution)/shard_map/ppermute | solution.py:16
  316.8 4.8 %slice-start.6 = ((s8[6291456]{0:T(1024)(128)(4,1)}), s8[4194304]{0:T(1024)(128)(4,1)S(1)}, s32[]{:S(2)}) async-start(s8[6291456]{0:T(1024)(128)(4,1)} %bitcast.22), calls=%async_computation.6 | async-start | bytes 8388608
  (6 other events, 14.1 us)
